TPU v7x, 32 devices: a whole 2x2x4 slice. The times are simulated.
32 devices in a mesh: replica: 8 (over z, x), tensor: 4 (over y, core).
Axes of the slice: x: 2, y: 2, z: 4, core: 2. Of those that a mesh axis runs over, the one named last changes fastest.
Arguments:
- hidden: bfloat16 [256, 8192], P('replica', 'tensor'), may hold values from -600 to 600
- input_norm_gain: float32 [8192], replicated, may hold values from 0.1 to 1.9
- key_value_weight: bfloat16 [8192, 2, 1024], P(None, None, 'tensor'), may hold values from -0.0625 to 0.0625
- adapter_down: bfloat16 [128, 8192, 128], P('replica', 'tensor'), may hold values from -0.0625 to 0.0625
- adapter_up: bfloat16 [128, 2, 64, 1024], P('replica', None, None, 'tensor'), may hold values from -0.75 to 0.75
- query: bfloat16 [256, 8192], P('replica', 'tensor'), may hold values from -6 to 6
- key_value_cache: bfloat16 [256, 512, 2, 1024], P('replica', None, None, 'tensor'), may hold values from -6 to 6
- segment_adapter: int32 [8, 16], P('replica'), may hold values from 0 to 127, as said below
- segment_sizes: int32 [8, 16], P('replica'), may hold values from 1 to 4, 32 in all within a row
- cached_length: int32 [256], P('replica'), may hold values from 2 to 512, as said below
Outputs:
- new_kv: bfloat16 [256, 2, 1024], P('replica', None, 'tensor')
- attended: bfloat16 [256, 8192], P('replica', 'tensor')
Inputs may be any that keep to these rules, and one draw needn't show every extreme that they name: `segment_adapter`: the segments of one replica name distinct adapters; adapter a is stored at index a // 16 of replica. At most 2 of one replica's segments name adapters stored at one index of replica, and in every replica's list some index of replica is named exactly 2 times. `segment_sizes`: the sizes of one replica's segments sum to 32. The new token takes position cached_length.
All inputs are finite; a program needn't handle non-finite values.
Results may differ from a plain program's by a relative error of at most 0.0058.
Values may be sent and summed in bfloat16 or wider, within the bound.
No kernel may reach another device: no remote copies, remote signals or barrier semaphores. Data moves between devices by JAX's collectives and lax.ppermute only.
A program may use at most 192 MiB of HBM per device.

v0:
```python
import jax
import jax.numpy as jnp
from jax import lax
from jax.sharding import PartitionSpec as P

HEAD = 128
ADP_DEV = 16
SLOT = 4
CAP = 2
ADAPTER_SCALE = 0.5
ROPE_BASE = 500000.0
EPSILON = 1e-05


def rotate(key_heads, token_position):
    half_size = key_heads.shape[-1] // 2
    inv_freq = ROPE_BASE ** (
        -(jnp.arange(half_size, dtype=jnp.float32) * 2.0) / key_heads.shape[-1]
    )
    angles = token_position.astype(jnp.float32)[:, None] * inv_freq[None, :]
    cosine_term = jnp.cos(angles)[:, None, :]
    sine_term = jnp.sin(angles)[:, None, :]
    first_half = key_heads[..., :half_size]
    second_half = key_heads[..., half_size:]
    return jnp.concatenate(
        [
            first_half * cosine_term - second_half * sine_term,
            second_half * cosine_term + first_half * sine_term,
        ],
        axis=-1,
    )


def body(
    hidden,
    input_norm_gain,
    key_value_weight,
    adapter_down,
    adapter_up,
    query,
    key_value_cache,
    segment_adapter,
    segment_sizes,
    cached_length,
):
    row_count = hidden.shape[0]
    part_width = hidden.shape[1]
    kv_width = key_value_weight.shape[2]
    kv_local = kv_width // HEAD
    cache_len = key_value_cache.shape[1]
    adapter_rank_size = adapter_up.shape[2]
    replicas = lax.axis_size("replica")
    segments = segment_sizes.shape[1]
    gathered = lax.all_gather(hidden, "tensor", axis=1, tiled=True)
    widened = gathered.astype(jnp.float32)
    normed = (
        widened
        * lax.rsqrt(jnp.mean(widened * widened, axis=1, keepdims=True) + EPSILON)
        * input_norm_gain
    ).astype(jnp.bfloat16)
    own_cols = lax.dynamic_slice_in_dim(
        normed, lax.axis_index("tensor") * part_width, part_width, 1
    )
    seg_counts = segment_sizes[0]
    adapters = segment_adapter[0]
    seg_ends = jnp.cumsum(seg_counts, dtype=jnp.int32)
    starts = seg_ends - seg_counts
    offsets = jnp.arange(SLOT, dtype=jnp.int32)
    row_ids = jnp.arange(row_count, dtype=jnp.int32)
    segment_index = jnp.sum((seg_ends[None, :] <= row_ids[:, None]).astype(jnp.int32), axis=1)
    token_position = row_ids - starts[segment_index]
    owners = adapters // ADP_DEV
    local_ids = adapters % ADP_DEV
    seg_ids = jnp.arange(segments, dtype=jnp.int32)
    slot_rank = jnp.sum(
        ((owners[None, :] == owners[:, None]) & (seg_ids[None, :] < seg_ids[:, None])).astype(
            jnp.int32
        ),
        axis=1,
    )
    owner_hit = (owners[None, None, :] == jnp.arange(replicas, dtype=jnp.int32)[:, None, None]) & (
        slot_rank[None, None, :] == jnp.arange(CAP, dtype=jnp.int32)[None, :, None]
    )
    wanted = jnp.sum(jnp.where(owner_hit, local_ids[None, None, :], 0), axis=2)
    fetch_slot = owners * CAP + slot_rank
    seg_at = jnp.sum(jnp.where(owner_hit, seg_ids[None, None, :], 0), axis=2)
    filled = jnp.any(owner_hit, axis=2)
    slot_counts = jnp.where(filled, seg_counts[seg_at], 0)
    slot_live = offsets[None, None, :] < slot_counts[:, :, None]
    source_row = jnp.where(slot_live, starts[seg_at][:, :, None] + offsets[None, None, :], 0)
    slot_rows = jnp.where(
        slot_live[:, :, :, None], own_cols[source_row], jnp.zeros((), jnp.bfloat16)
    )
    segment_member_mask = lax.all_to_all(wanted, "replica", split_axis=0, concat_axis=0, tiled=True)
    selected_down = adapter_down[segment_member_mask]
    selected_up = adapter_up[segment_member_mask]
    down_got = lax.all_to_all(selected_down, "replica", split_axis=0, concat_axis=0, tiled=True)
    up_got = lax.all_to_all(selected_up, "replica", split_axis=0, concat_axis=0, tiled=True)
    partial_value = jnp.einsum(
        "oksd,okdr->oksr", slot_rows, down_got, preferred_element_type=jnp.float32
    )
    summed = lax.psum(partial_value, "tensor").astype(jnp.bfloat16)
    summed = summed.reshape(summed.shape[:3] + (2, adapter_rank_size))
    slot_delta = (
        jnp.einsum("okscr,okcrw->okscw", summed, up_got, preferred_element_type=jnp.float32)
        * ADAPTER_SCALE
    )
    flat_delta = slot_delta.reshape((replicas * CAP * SLOT,) + slot_delta.shape[3:])
    adapter_delta = flat_delta[fetch_slot[segment_index] * SLOT + token_position]
    base_projection = jnp.dot(
        normed,
        key_value_weight.reshape(key_value_weight.shape[0], 2 * kv_width),
        preferred_element_type=jnp.float32,
    ).reshape(row_count, 2, kv_width)
    current_key_value = base_projection + adapter_delta
    rotated = rotate(
        current_key_value[:, 0].reshape(row_count, kv_local, HEAD), cached_length
    ).reshape(row_count, kv_width)
    new_kv = jnp.stack([rotated, current_key_value[:, 1]], axis=1).astype(jnp.bfloat16)
    group_size = query.shape[1] // HEAD // kv_local
    scale = float(HEAD) ** (-0.5)
    query_heads = query.reshape(row_count, kv_local, group_size, HEAD)
    cached_keys = key_value_cache[:, :, 0].reshape(row_count, cache_len, kv_local, HEAD)
    cached_values = key_value_cache[:, :, 1].reshape(row_count, cache_len, kv_local, HEAD)
    scores = (
        jnp.einsum("bhgd,bthd->bhgt", query_heads, cached_keys, preferred_element_type=jnp.float32)
        * scale
    )
    is_live = jnp.arange(cache_len, dtype=jnp.int32)[None, :] < cached_length[:, None]
    scores = jnp.where(is_live[:, None, None, :], scores, -jnp.inf)
    new_key = new_kv[:, 0].reshape(row_count, kv_local, HEAD)
    new_value = new_kv[:, 1].astype(jnp.float32).reshape(row_count, kv_local, HEAD)
    own_score = (
        jnp.einsum("bhgd,bhd->bhg", query_heads, new_key, preferred_element_type=jnp.float32)
        * scale
    )
    top_score = jnp.maximum(jnp.max(scores, axis=-1), own_score)
    weights = jnp.exp(scores - top_score[..., None])
    own_weight = jnp.exp(own_score - top_score)
    total_mass = jnp.sum(weights, axis=-1) + own_weight
    prob_rows = (weights / total_mass[..., None]).astype(jnp.bfloat16)
    own_prob = (own_weight / total_mass).astype(jnp.bfloat16)
    context = jnp.einsum(
        "bhgt,bthd->bhgd", prob_rows, cached_values, preferred_element_type=jnp.float32
    )
    context = context + own_prob.astype(jnp.float32)[..., None] * new_value[:, :, None, :]
    attended = context.reshape(row_count, kv_local * group_size * HEAD).astype(jnp.bfloat16)
    return (new_kv, attended)


def solution(mesh):
    in_specs = (
        P("replica", "tensor"),
        P(),
        P(None, None, "tensor"),
        P("replica", "tensor", None),
        P("replica", None, None, "tensor"),
        P("replica", "tensor"),
        P("replica", None, None, "tensor"),
        P("replica", None),
        P("replica", None),
        P("replica"),
    )
    out_specs = (P("replica", None, "tensor"), P("replica", "tensor"))
    return jax.shard_map(body, mesh=mesh, in_specs=in_specs, out_specs=out_specs, check_vma=False)
```

profile of v0, /device:TPU:0, one launch (start us, length us, event | category | flops | bytes accessed | tf_op | source)
XLA Modules:
  0.0 256.9 jit_solution(18434199444916356622)
XLA Ops:
  0.6 0.8 fusion.26
  1.4 0.7 and_select_fusion.2
  2.1 0.2 convert_reduce_fusion.1
  2.3 0.1 fusion.18
  2.4 0.1 copy.82
  2.5 13.5 %all_to_all.22 = s32[8,1,2]{2,1,0:T(1,128)S(1)} all-to-all(s32[8,1,2]{2,1,0:T(1,128)S(1)} %copy.82), channel_id=1, replica_groups=mesh['replica'=8,'tensor'=4] {'replica'}, dimensions={0} | all-to-all | bytes 128 | tf_op jit(solution)/shard_map/all_to_all | solution.py:94
  16.0 0.1 copy.83
  16.1 0.1 copy.84
  16.2 0.1 reshape.385
  16.3 8.1 %gather_fusion.4 = bf16[16,2048,128]{2,1,0:T(8,128)(2,1)} fusion(bf16[16,2048,128]{2,1,0:T(8,128)(2,1)} %param.13, s32[1024]{0:T(1024)S(1)} %pad_clamp_fusion.4), kind=kCustom, calls=%fused_computation.4 | custom fusion | bytes 16777280 | tf_op jit(solution)/shard_map/gather | solution.py:95
  24.4 5.0 %all-to-all-start.2 = ((bf16[8,2,2048,128]{3,2,1,0:T(8,128)(2,1)}), bf16[8,2,2048,128]{3,2,1,0:T(8,128)(2,1)}, u32[]{:S(2)}, u32[]{:S(2)}) async-start(bf16[8,2,2048,128]{3,2,1,0:T(8,128)(2,1)} %bitcast.100), calls=%async_computation.2 | async-start | bytes 16777216 | tf_op jit(solution)/shard_map/all_to_all | solution.py:97
  29.4 8.0 %copy.109 = bf16[1024,8,2,256]{3,1,2,0:T(8,128)(2,1)} copy(bf16[1024,8,2,256]{3,2,1,0:T(2,128)(2,1)} %bitcast.104) | data formatting | bytes 16777216
  37.4 11.3 %copy.81 = bf16[512,8192]{1,0:T(8,128)(2,1)} copy(bf16[512,8192]{0,1:T(8,128)(2,1)} %bitcast.102) | data formatting | bytes 16777216 | tf_op jit(solution)/shard_map/dot_general | solution.py:110
  48.7 0.1 copy.89
  48.9 0.1 reduce
  49.0 0.1 copy.85
  49.1 0.1 reshape.393
  49.2 0.7 gather_fusion.2
  49.8 0.1 reshape.400
  49.9 0.7 gather_fusion.1
  50.7 0.1 copy.86
  50.8 0.2 and_reduce_fusion
  50.9 0.1 copy.87
  51.0 0.1 compare_select_fusion
  51.1 0.1 reshape.409
  51.2 7.2 %all_gather.3 = bf16[32,8192]{1,0:T(8,128)(2,1)S(1)} all-gather(bf16[32,2048]{1,0:T(8,128)(2,1)S(1)} %copy-done.3), channel_id=1, replica_groups=mesh['replica'=8,'tensor'=4] {'tensor'}, dimensions={1}, use_global_device_ids=true | all-gather | bytes 655360 | tf_op jit(solution)/shard_map/all_gather | solution.py:54
  58.4 0.2 fusion.3
  58.7 0.2 fusion.5
  58.9 0.8 copy-done.2
  59.7 0.7 gather_fusion.3
  60.4 0.1 reshape.408
  60.5 0.1 convert_reduce_fusion
  60.6 1.3 gather_fusion.6
  61.9 1.3 gather_fusion.5
  63.2 0.5 convert_element_type.49
  63.7 33.0 %fusion.28 = (bf16[32,512,1,256]{3,2,1,0:T(2,128)(2,1)}, bf16[32,512,1,256]{3,2,1,0:T(2,128)(2,1)}) fusion(bf16[32,512,2,256]{3,2,1,0:T(2,128)(2,1)} %param.16), kind=kLoop, calls=%fused_computation.94 | loop fusion | bytes 33554432 | tf_op jit(solution)/shard_map/slice | solution.py:123
  96.7 35.5 %copy.108 = bf16[32,512,1,256]{1,3,0,2:T(8,128)(2,1)} copy(bf16[32,512,1,256]{3,2,1,0:T(2,128)(2,1)} %get-tuple-element.17) | data formatting | bytes 16777216
  132.2 35.6 %copy.107 = bf16[32,512,1,256]{1,3,0,2:T(8,128)(2,1)} copy(bf16[32,512,1,256]{3,2,1,0:T(2,128)(2,1)} %get-tuple-element.16) | data formatting | bytes 16777216
  167.8 0.1 iota_compare_fusion
  167.9 1.7 gather_fusion
  169.6 41.7 %all-to-all-done.2 = bf16[8,2,2048,128]{3,2,1,0:T(8,128)(2,1)} async-done(((bf16[8,2,2048,128]{3,2,1,0:T(8,128)(2,1)}), bf16[8,2,2048,128]{3,2,1,0:T(8,128)(2,1)}, u32[]{:S(2)}, u32[]{:S(2)}) %all-to-all-start.2) | async-done | bytes 8388640 | tf_op jit(solution)/shard_map/all_to_all | solution.py:97
  211.3 3.6 %all-to-all-start.1 = ((bf16[8,2,2,64,256]{4,3,2,1,0:T(8,128)(2,1)}), bf16[8,2,2,64,256]{4,3,2,1,0:T(8,128)(2,1)S(1)}, u32[]{:S(2)}, u32[]{:S(2)}) async-start(bf16[8,2,2,64,256]{4,3,2,1,0:T(8,128)(2,1)} %bitcast.7), calls=%async_computation.1 | async-start | bytes 2097152 | tf_op jit(solution)/shard_map/all_to_all | solution.py:98
  214.9 5.3 %fusion.29 = (f32[32,2,8]{2,1,0:T(2,128)}, f32[32,2,8,512]{3,2,1,0:T(8,128)S(1)}) fusion(bf16[32,2,8,128]{3,2,1,0:T(8,128)(2,1)S(1)} %bitcast.105, bf16[32,512,2,128]{1,3,2,0:T(8,128)(2,1)} %bitcast.99, pred[32,512]{1,0:T(8,128)(4,1)S(1)} %iota_compare_fusion), kind=kOutput, calls=%fused_computation.95 | convolution fusion | flops 67894784 | bytes 9586688 | tf_op jit(solution)/shard_map/bhgd,bthd->bhgt/dot_general | solution.py:126
  220.2 0.8 copy.95
  221.0 0.7 fusion.24
  221.7 0.8 iota_compare_fusion.2
  222.5 1.4 multiply_cosine_fusion
  223.8 5.2 %fusion.10 = f32[8,2,4,128]{3,2,1,0:T(4,128)} fusion(bf16[8,2,2048,128]{3,2,1,0:T(8,128)(2,1)} %all-to-all-done.2, bf16[8,2,4,2048]{3,2,1,0:T(4,128)(2,1)S(1)} %reshape.408, pred[8,2,4]{2,1,0:T(4,128)(4,1)S(1)} %iota_compare_fusion.2), kind=kOutput, calls=%fused_computation.26 | convolution fusion | flops 33685504 | bytes 8683584 | tf_op jit(solution)/shard_map/oksd,okdr->oksr/dot_general | solution.py:99
  229.1 12.1 %psum.7 = bf16[8,2,4,128]{3,2,1,0:T(4,128)(2,1)S(1)} all-reduce(f32[8,2,4,128]{3,2,1,0:T(4,128)} %fusion.10), channel_id=1, replica_groups=mesh['replica'=8,'tensor'=4] {'tensor'}, use_global_device_ids=true, to_apply=%region_6.7 | all-reduce | flops 8192 | bytes 49152 | tf_op jit(solution)/shard_map/psum | solution.py:102
  241.2 0.1 reshape.379
  241.2 0.2 fusion.2
  241.6 0.6 gather_fusion.7
  242.2 6.2 %convolution_add_fusion.1 = f32[32,2,256]{2,0,1:T(8,128)S(1)} fusion(bf16[2,256,8192]{2,1,0:T(8,128)(2,1)} %bitcast.101, bf16[32,8192]{1,0:T(8,128)(2,1)} %copy-done.2, f32[32,2,256]{2,1,0:T(2,128)S(1)} %gather_fusion.7), kind=kOutput, calls=%fused_computation.16 | convolution fusion | flops 268451840 | bytes 9043968 | tf_op jit(solution)/shard_map/dot_general | solution.py:110
  248.5 0.1 subtract_convert_fusion
  248.6 0.1 pad_maximum_fusion.1
  248.7 0.1 fusion.37
  248.8 0.6 copy.102
  249.5 0.2 fusion.15
  249.8 0.1 copy.96
  249.9 0.4 fusion.6
  250.3 0.1 copy.98
  250.4 0.1 copy.101
  250.5 5.7 %fusion.1 = bf16[32,2,8,128]{3,2,1,0:T(8,128)(2,1)S(1)} fusion(bf16[32,512,2,128]{1,3,2,0:T(8,128)(2,1)} %bitcast.103, f32[32,2,8,512]{3,2,1,0:T(8,128)S(1)} %get-tuple-element.27, f32[32,2,8]{2,1,0:T(2,128)S(1)} %copy.98, f32[32,2,8]{2,1,0:T(2,128)S(1)} %copy.96, f32[32,2,128]{2,1,0:T(2,128)S(1)} %reshape.382, f32[32,2,8]{2,1,0:T(2,128)S(1)} %copy.101), kind=kOutput, calls=%fused_computation.13 | convolution fusion | flops 68091904 | bytes 9607168 | tf_op jit(solution)/shard_map/bhgt,bthd->bhgd/dot_general | solution.py:143
  256.2 0.7 copy.118
  (50 shorter events, 0.6 us)
Async XLA Ops:
  0.6 167.3 %copy-start = (bf16[16,2,64,256]{3,2,1,0:T(8,128)(2,1)S(1)}, bf16[16,2,64,256]{3,2,1,0:T(8,128)(2,1)}, u32[]{:S(2)}) copy-start(bf16[16,2,64,256]{3,2,1,0:T(8,128)(2,1)} %param.14) | copy-start | bytes 3145732
  24.4 186.9 %all-to-all-start.2 = ((bf16[8,2,2048,128]{3,2,1,0:T(8,128)(2,1)}), bf16[8,2,2048,128]{3,2,1,0:T(8,128)(2,1)}, u32[]{:S(2)}, u32[]{:S(2)}) async-start(bf16[8,2,2048,128]{3,2,1,0:T(8,128)(2,1)} %bitcast.100), calls=%async_computation.2 | async-start | bytes 16777216 | tf_op jit(solution)/shard_map/all_to_all | solution.py:97
  37.4 11.4 %copy-start.1 = (s32[1,16]{1,0:T(1,128)S(1)}, s32[1,16]{1,0:T(1,128)}, u32[]{:S(2)}) copy-start(s32[1,16]{1,0:T(1,128)} %param.18) | copy-start | bytes 196
  48.7 2.5 copy-start.3
  48.7 9.9 %copy-start.8 = (f32[8192]{0:T(1024)S(1)}, f32[8192]{0:T(1024)}, u32[]{:S(2)}) copy-start(f32[8192]{0:T(1024)} %param.11) | copy-start | bytes 98308
  48.7 14.5 %copy-start.9 = (s32[32]{0:T(128)S(1)}, s32[32]{0:T(128)}, u32[]{:S(2)}) copy-start(s32[32]{0:T(128)} %param.19) | copy-start | bytes 388
  51.0 7.7 %copy-start.7 = (s32[8,2]{1,0:T(8,128)}, s32[8,2]{1,0:T(8,128)S(1)}, u32[]{:S(2)}) copy-start(s32[8,2]{1,0:T(8,128)S(1)} %copy.87) | copy-start | bytes 196
  58.9 0.8 copy-start.2
  96.7 35.5 %copy-start.4 = (bf16[32,2048]{1,0:T(8,128)(2,1)S(1)}, bf16[32,2048]{1,0:T(8,128)(2,1)}, u32[]{:S(2)}) copy-start(bf16[32,2048]{1,0:T(8,128)(2,1)} %param.15) | copy-start | bytes 393220
  211.3 30.0 %all-to-all-start.1 = ((bf16[8,2,2,64,256]{4,3,2,1,0:T(8,128)(2,1)}), bf16[8,2,2,64,256]{4,3,2,1,0:T(8,128)(2,1)S(1)}, u32[]{:S(2)}, u32[]{:S(2)}) async-start(bf16[8,2,2,64,256]{4,3,2,1,0:T(8,128)(2,1)} %bitcast.7), calls=%async_computation.1 | async-start | bytes 2097152 | tf_op jit(solution)/shard_map/all_to_all | solution.py:98
  229.1 19.4 %copy-start.5 = (f32[32,64]{1,0:T(8,128)S(1)}, f32[32,64]{1,0:T(8,128)}, u32[]{:S(2)}) copy-start(f32[32,64]{1,0:T(8,128)} %get-tuple-element.22) | copy-start | bytes 24580
  229.1 19.4 %copy-start.6 = (f32[32,64]{1,0:T(8,128)S(1)}, f32[32,64]{1,0:T(8,128)}, u32[]{:S(2)}) copy-start(f32[32,64]{1,0:T(8,128)} %get-tuple-element.23) | copy-start | bytes 24580
where the time goes:
time: 260 us; the launch traced here: 257 us
  local copies, waits for them, and re-layouts  143 us (55%)
  waiting for transfers between devices  41.7 us (16%)
  blocking collectives  32.8 us (13%)
  matrix products  22.9 us (9%)
  starting transfers between devices  8.57 us (3%)
  other arithmetic  6.85 us (3%)
    unnamed x26, local copies, waits for them, and re-layouts  81.3 us
    all_to_all x1, waiting for transfers between devices, body(): lax.all_to_all(selected_down, 'replica', split_axis=0, concat_axis=0, til...  41.7 us
    slice x1, local copies, waits for them, and re-layouts, body(): key_value_cache[:, :, 0].reshape(row_count, cache_len, kv_local, HEAD)  33 us
    all_to_all x1, blocking collectives, body(): lax.all_to_all(wanted, 'replica', split_axis=0, concat_axis=0, tiled=True)  13.5 us
    psum x1, blocking collectives, body(): summed = lax.psum(partial_value, 'tensor').astype(jnp.bfloat16)  12.1 us
    dot_general x1, local copies, waits for them, and re-layouts, body(): jnp.dot(normed, key_value_weight.reshape(key_value_weight.shape[0], 2 * k...  11.3 us
    gather x1, local copies, waits for them, and re-layouts, body(): selected_down = adapter_down[segment_member_mask]  8.13 us
    all_gather x1, blocking collectives, body(): gathered = lax.all_gather(hidden, 'tensor', axis=1, tiled=True)  7.2 us
  transfers between devices with their start and end apart: 2, of which 1 were waited for; matrix products, arithmetic and copies ran while one was open for 57% of the time, Pallas kernels for 0%

commit v1 on v0

--- a/solution.py
+++ b/solution.py
@@ -99,7 +99,7 @@
     partial_value = jnp.einsum(
         "oksd,okdr->oksr", slot_rows, down_got, preferred_element_type=jnp.float32
     )
-    summed = lax.psum(partial_value, "tensor").astype(jnp.bfloat16)
+    summed = jnp.sum(lax.all_gather(partial_value, "tensor"), axis=0).astype(jnp.bfloat16)
     summed = summed.reshape(summed.shape[:3] + (2, adapter_rank_size))
     slot_delta = (
         jnp.einsum("okscr,okcrw->okscw", summed, up_got, preferred_element_type=jnp.float32)

time: 260 us -> 259 us (level)
  waiting for transfers between devices: 41.7 us -> 48.1 us
  blocking collectives: 32.8 us -> 26.5 us
    psum x1 -> x0, blocking collectives: 12.1 us -> none  [body(): summed = lax.psum(partial_value, 'tensor').astype(jnp.bfloat16)]
    all_to_all x1, waiting for transfers between devices: 0.01 us -> 6.45 us  [body(): lax.all_to_all(selected_up, 'replica', split_axis=0, concat_axis=0, tiled...]
    all_gather x0 -> x1, blocking collectives: none -> 5.74 us  [body(): lax.all_gather(partial_value, 'tensor')]
  transfers between devices with their start and end apart: 2 -> 2, of which waited for: 1 -> 2; matrix products, arithmetic and copies ran while one was open for 57% -> 57% of each run, Pallas kernels for 0% -> 0%
where the time goes in v1:
time: 259 us; the launch traced here: 257 us
  local copies, waits for them, and re-layouts  143 us (55%)
  waiting for transfers between devices  48.1 us (19%)
  blocking collectives  26.5 us (10%)
  matrix products  22.2 us (9%)
  starting transfers between devices  8.57 us (3%)
  other arithmetic  6.99 us (3%)
    unnamed x26, local copies, waits for them, and re-layouts  81.3 us
    all_to_all x1, waiting for transfers between devices, body(): lax.all_to_all(selected_down, 'replica', split_axis=0, concat_axis=0, til...  41.7 us
    slice x1, local copies, waits for them, and re-layouts, body(): key_value_cache[:, :, 0].reshape(row_count, cache_len, kv_local, HEAD)  33 us
    all_to_all x1, blocking collectives, body(): lax.all_to_all(wanted, 'replica', split_axis=0, concat_axis=0, tiled=True)  13.5 us
    dot_general x1, local copies, waits for them, and re-layouts, body(): jnp.dot(normed, key_value_weight.reshape(key_value_weight.shape[0], 2 * k...  11.3 us
    gather x1, local copies, waits for them, and re-layouts, body(): selected_down = adapter_down[segment_member_mask]  8.13 us
    all_gather x1, blocking collectives, body(): gathered = lax.all_gather(hidden, 'tensor', axis=1, tiled=True)  7.2 us
    all_to_all x1, waiting for transfers between devices, body(): lax.all_to_all(selected_up, 'replica', split_axis=0, concat_axis=0, tiled...  6.45 us
  transfers between devices with their start and end apart: 2, of which 2 were waited for; matrix products, arithmetic and copies ran while one was open for 57% of the time, Pallas kernels for 0%

profile of v1, /device:TPU:0, one launch (start us, length us, event | category | flops | bytes accessed | tf_op | source)
XLA Modules:
  0.0 256.5 jit_solution(3242119431928728630)
XLA Ops:
  0.6 0.8 fusion.26
  1.4 0.7 and_select_fusion.2
  2.1 0.2 convert_reduce_fusion.1
  2.3 0.1 fusion.18
  2.4 0.1 copy.84
  2.5 13.5 %all_to_all.22 = s32[8,1,2]{2,1,0:T(1,128)S(1)} all-to-all(s32[8,1,2]{2,1,0:T(1,128)S(1)} %copy.84), channel_id=1, replica_groups=mesh['replica'=8,'tensor'=4] {'replica'}, dimensions={0} | all-to-all | bytes 128 | tf_op jit(solution)/shard_map/all_to_all | solution.py:94
  16.0 0.1 copy.85
  16.1 0.1 copy.86
  16.2 0.1 reshape.384
  16.3 8.1 %gather_fusion.4 = bf16[16,2048,128]{2,1,0:T(8,128)(2,1)} fusion(bf16[16,2048,128]{2,1,0:T(8,128)(2,1)} %param.13, s32[1024]{0:T(1024)S(1)} %pad_clamp_fusion.4), kind=kCustom, calls=%fused_computation.4 | custom fusion | bytes 16777280 | tf_op jit(solution)/shard_map/gather | solution.py:95
  24.4 5.0 %all-to-all-start.2 = ((bf16[8,2,2048,128]{3,2,1,0:T(8,128)(2,1)}), bf16[8,2,2048,128]{3,2,1,0:T(8,128)(2,1)}, u32[]{:S(2)}, u32[]{:S(2)}) async-start(bf16[8,2,2048,128]{3,2,1,0:T(8,128)(2,1)} %bitcast.101), calls=%async_computation.2 | async-start | bytes 16777216 | tf_op jit(solution)/shard_map/all_to_all | solution.py:97
  29.4 8.0 %copy.114 = bf16[1024,8,2,256]{3,1,2,0:T(8,128)(2,1)} copy(bf16[1024,8,2,256]{3,2,1,0:T(2,128)(2,1)} %bitcast.105) | data formatting | bytes 16777216
  37.4 11.3 %copy.83 = bf16[512,8192]{1,0:T(8,128)(2,1)} copy(bf16[512,8192]{0,1:T(8,128)(2,1)} %bitcast.103) | data formatting | bytes 16777216 | tf_op jit(solution)/shard_map/dot_general | solution.py:110
  48.7 0.1 copy.91
  48.9 0.1 reduce
  49.0 0.1 copy.87
  49.1 0.1 reshape.392
  49.2 0.7 gather_fusion.2
  49.8 0.1 reshape.399
  49.9 0.7 gather_fusion.1
  50.7 0.1 copy.88
  50.8 0.2 and_reduce_fusion
  50.9 0.1 copy.89
  51.0 0.1 compare_select_fusion
  51.1 0.1 reshape.408
  51.2 7.2 %all_gather.9 = bf16[32,8192]{1,0:T(8,128)(2,1)S(1)} all-gather(bf16[32,2048]{1,0:T(8,128)(2,1)S(1)} %copy-done.3), channel_id=1, replica_groups=mesh['replica'=8,'tensor'=4] {'tensor'}, dimensions={1}, use_global_device_ids=true | all-gather | bytes 655360 | tf_op jit(solution)/shard_map/all_gather | solution.py:54
  58.4 0.2 fusion.3
  58.7 0.2 fusion.5
  58.9 0.8 copy-done.2
  59.7 0.7 gather_fusion.3
  60.4 0.1 reshape.407
  60.5 0.1 convert_reduce_fusion
  60.6 1.2 gather_fusion.6
  61.9 1.3 gather_fusion.5
  63.2 0.6 convert_element_type.54
  63.7 33.0 %fusion.28 = (bf16[32,512,1,256]{3,2,1,0:T(2,128)(2,1)}, bf16[32,512,1,256]{3,2,1,0:T(2,128)(2,1)}) fusion(bf16[32,512,2,256]{3,2,1,0:T(2,128)(2,1)} %param.16), kind=kLoop, calls=%fused_computation.94 | loop fusion | bytes 33554432 | tf_op jit(solution)/shard_map/slice | solution.py:123
  96.7 35.5 %copy.113 = bf16[32,512,1,256]{1,3,0,2:T(8,128)(2,1)} copy(bf16[32,512,1,256]{3,2,1,0:T(2,128)(2,1)} %get-tuple-element.17) | data formatting | bytes 16777216
  132.2 35.6 %copy.112 = bf16[32,512,1,256]{1,3,0,2:T(8,128)(2,1)} copy(bf16[32,512,1,256]{3,2,1,0:T(2,128)(2,1)} %get-tuple-element.16) | data formatting | bytes 16777216
  167.9 1.7 gather_fusion
  169.6 41.7 %all-to-all-done.2 = bf16[8,2,2048,128]{3,2,1,0:T(8,128)(2,1)} async-done(((bf16[8,2,2048,128]{3,2,1,0:T(8,128)(2,1)}), bf16[8,2,2048,128]{3,2,1,0:T(8,128)(2,1)}, u32[]{:S(2)}, u32[]{:S(2)}) %all-to-all-start.2) | async-done | bytes 8388640 | tf_op jit(solution)/shard_map/all_to_all | solution.py:97
  211.3 3.6 %all-to-all-start.1 = ((bf16[8,2,2,64,256]{4,3,2,1,0:T(8,128)(2,1)}), bf16[8,2,2,64,256]{4,3,2,1,0:T(8,128)(2,1)S(1)}, u32[]{:S(2)}, u32[]{:S(2)}) async-start(bf16[8,2,2,64,256]{4,3,2,1,0:T(8,128)(2,1)} %bitcast.7), calls=%async_computation.1 | async-start | bytes 2097152 | tf_op jit(solution)/shard_map/all_to_all | solution.py:98
  214.9 5.3 %fusion.29 = (f32[32,2,8]{2,1,0:T(2,128)}, f32[32,2,8,512]{3,2,1,0:T(8,128)S(1)}) fusion(bf16[32,2,8,128]{3,2,1,0:T(8,128)(2,1)S(1)} %bitcast.106, bf16[32,512,2,128]{1,3,2,0:T(8,128)(2,1)} %bitcast.100, pred[32,512]{1,0:T(8,128)(4,1)S(1)} %iota_compare_fusion), kind=kOutput, calls=%fused_computation.95 | convolution fusion | flops 67894784 | bytes 9586688 | tf_op jit(solution)/shard_map/bhgd,bthd->bhgt/dot_general | solution.py:126
  220.2 0.8 copy.98
  221.0 0.7 fusion.24
  221.7 0.8 iota_compare_fusion.2
  222.5 1.4 multiply_cosine_fusion
  223.9 4.6 %fusion.10 = f32[8,2,4,128]{3,2,1,0:T(4,128)S(1)} fusion(bf16[8,2,2048,128]{3,2,1,0:T(8,128)(2,1)} %all-to-all-done.2, bf16[8,2,4,2048]{3,2,1,0:T(4,128)(2,1)S(1)} %reshape.407, pred[8,2,4]{2,1,0:T(4,128)(4,1)S(1)} %iota_compare_fusion.2), kind=kOutput, calls=%fused_computation.26 | convolution fusion | flops 33685504 | bytes 8683584 | tf_op jit(solution)/shard_map/oksd,okdr->oksr/dot_general | solution.py:99
  228.5 5.7 %all-gather = f32[32,2,4,128]{3,2,1,0:T(4,128)S(1)} all-gather(f32[8,2,4,128]{3,2,1,0:T(4,128)S(1)} %fusion.10), channel_id=2, replica_groups=mesh['replica'=8,'tensor'=4] {'tensor'}, dimensions={0}, use_global_device_ids=true | all-gather | bytes 163840 | tf_op jit(solution)/shard_map/all_gather | solution.py:102
  234.3 0.1 reshape.455
  234.4 6.4 %all-to-all-done.1 = bf16[8,2,2,64,256]{4,3,2,1,0:T(8,128)(2,1)S(1)} async-done(((bf16[8,2,2,64,256]{4,3,2,1,0:T(8,128)(2,1)}), bf16[8,2,2,64,256]{4,3,2,1,0:T(8,128)(2,1)S(1)}, u32[]{:S(2)}, u32[]{:S(2)}) %all-to-all-start.1) | async-done | bytes 1048608 | tf_op jit(solution)/shard_map/all_to_all | solution.py:98
  240.8 0.2 fusion.2
  241.2 0.6 gather_fusion.7
  241.8 6.2 %convolution_add_fusion.1 = f32[32,2,256]{2,0,1:T(8,128)S(1)} fusion(bf16[2,256,8192]{2,1,0:T(8,128)(2,1)} %bitcast.102, bf16[32,8192]{1,0:T(8,128)(2,1)} %copy-done.2, f32[32,2,256]{2,1,0:T(2,128)S(1)} %gather_fusion.7), kind=kOutput, calls=%fused_computation.16 | convolution fusion | flops 268451840 | bytes 9043968 | tf_op jit(solution)/shard_map/dot_general | solution.py:110
  248.1 0.1 subtract_convert_fusion
  248.2 0.1 pad_maximum_fusion.1
  248.3 0.1 fusion.37
  248.4 0.6 copy.105
  249.1 0.2 fusion.15
  249.4 0.1 copy.99
  249.5 0.4 fusion.6
  249.9 0.1 copy.101
  250.0 0.1 copy.104
  250.1 5.7 %fusion.1 = bf16[32,2,8,128]{3,2,1,0:T(8,128)(2,1)S(1)} fusion(bf16[32,512,2,128]{1,3,2,0:T(8,128)(2,1)} %bitcast.104, f32[32,2,8,512]{3,2,1,0:T(8,128)S(1)} %get-tuple-element.27, f32[32,2,8]{2,1,0:T(2,128)S(1)} %copy.101, f32[32,2,8]{2,1,0:T(2,128)S(1)} %copy.99, f32[32,2,128]{2,1,0:T(2,128)S(1)} %reshape.381, f32[32,2,8]{2,1,0:T(2,128)S(1)} %copy.104), kind=kOutput, calls=%fused_computation.13 | convolution fusion | flops 68091904 | bytes 9607168 | tf_op jit(solution)/shard_map/bhgt,bthd->bhgd/dot_general | solution.py:143
  255.8 0.7 copy.123
  (51 shorter events, 0.7 us)
Async XLA Ops:
  0.6 167.3 %copy-start = (bf16[16,2,64,256]{3,2,1,0:T(8,128)(2,1)S(1)}, bf16[16,2,64,256]{3,2,1,0:T(8,128)(2,1)}, u32[]{:S(2)}) copy-start(bf16[16,2,64,256]{3,2,1,0:T(8,128)(2,1)} %param.14) | copy-start | bytes 3145732
  24.4 186.9 %all-to-all-start.2 = ((bf16[8,2,2048,128]{3,2,1,0:T(8,128)(2,1)}), bf16[8,2,2048,128]{3,2,1,0:T(8,128)(2,1)}, u32[]{:S(2)}, u32[]{:S(2)}) async-start(bf16[8,2,2048,128]{3,2,1,0:T(8,128)(2,1)} %bitcast.101), calls=%async_computation.2 | async-start | bytes 16777216 | tf_op jit(solution)/shard_map/all_to_all | solution.py:97
  37.4 11.4 %copy-start.1 = (s32[1,16]{1,0:T(1,128)S(1)}, s32[1,16]{1,0:T(1,128)}, u32[]{:S(2)}) copy-start(s32[1,16]{1,0:T(1,128)} %param.18) | copy-start | bytes 196
  48.7 2.5 copy-start.3
  48.7 9.9 %copy-start.8 = (f32[8192]{0:T(1024)S(1)}, f32[8192]{0:T(1024)}, u32[]{:S(2)}) copy-start(f32[8192]{0:T(1024)} %param.11) | copy-start | bytes 98308
  48.7 14.4 %copy-start.9 = (s32[32]{0:T(128)S(1)}, s32[32]{0:T(128)}, u32[]{:S(2)}) copy-start(s32[32]{0:T(128)} %param.19) | copy-start | bytes 388
  51.0 7.7 %copy-start.7 = (s32[8,2]{1,0:T(8,128)}, s32[8,2]{1,0:T(8,128)S(1)}, u32[]{:S(2)}) copy-start(s32[8,2]{1,0:T(8,128)S(1)} %copy.89) | copy-start | bytes 196
  58.9 0.8 copy-start.2
  96.7 35.5 %copy-start.4 = (bf16[32,2048]{1,0:T(8,128)(2,1)S(1)}, bf16[32,2048]{1,0:T(8,128)(2,1)}, u32[]{:S(2)}) copy-start(bf16[32,2048]{1,0:T(8,128)(2,1)} %param.15) | copy-start | bytes 393220
  211.3 29.6 %all-to-all-start.1 = ((bf16[8,2,2,64,256]{4,3,2,1,0:T(8,128)(2,1)}), bf16[8,2,2,64,256]{4,3,2,1,0:T(8,128)(2,1)S(1)}, u32[]{:S(2)}, u32[]{:S(2)}) async-start(bf16[8,2,2,64,256]{4,3,2,1,0:T(8,128)(2,1)} %bitcast.7), calls=%async_computation.1 | async-start | bytes 2097152 | tf_op jit(solution)/shard_map/all_to_all | solution.py:98
  228.5 19.5 %copy-start.5 = (f32[32,64]{1,0:T(8,128)S(1)}, f32[32,64]{1,0:T(8,128)}, u32[]{:S(2)}) copy-start(f32[32,64]{1,0:T(8,128)} %get-tuple-element.22) | copy-start | bytes 24580
  228.5 19.5 %copy-start.6 = (f32[32,64]{1,0:T(8,128)S(1)}, f32[32,64]{1,0:T(8,128)}, u32[]{:S(2)}) copy-start(f32[32,64]{1,0:T(8,128)} %get-tuple-element.23) | copy-start | bytes 24580
